TPU v7x, 256 devices: a whole 4x4x8 slice. The times are simulated.
256 devices in a mesh: row: 32 (over y, x, core), col: 8 (over z).
Axes of the slice: x: 4, y: 4, z: 8, core: 2. Of those that a mesh axis runs over, the one named last changes fastest.
Arguments:
- covariance: float32 [8192, 8192], P('row', 'col'), may hold values from 0 to 4, as said below
- panels: int32 [4], replicated, may hold values from 0 to 31, as said below
- observed: float32 [8192], P('row'), may hold values from -6 to 6
- drift_basis: float32 [64, 8192], P(None, 'row'), may hold values from -1.5 to 1.5
Outputs:
- complement: float32 [8192, 8192], P('row', 'col')
- factor: float32 [8192, 1024], P('row')
- solved_data: float32 [8192], P('row')
- solved_drift: float32 [64, 8192], P(None, 'row')
Inputs may be any that keep to these rules, and one draw needn't show every extreme that they name: `covariance`: symmetric and positive definite. `panels`: 4 different tile indices; tile 32 - 1 is always among them.
All inputs are finite; a program needn't handle non-finite values.
Results may differ from a plain program's by a relative error of at most 0.0003.
Values sent between devices are 32-bit elements; how exact they have to be, the bound alone decides.
No kernel may reach another device: no remote copies, remote signals or barrier semaphores. Data moves between devices by JAX's collectives and lax.ppermute only.
A program may use at most 64 MiB of HBM per device.

v0:
```python
import jax
import jax.numpy as jnp
from jax import lax
from jax.sharding import PartitionSpec as P

B = 256
K = 4


def from_root(value, axis, root):
    return lax.dynamic_index_in_dim(lax.all_gather(value, axis), root, 0, keepdims=False)


def broadcast(value, axis, root):
    mine = lax.axis_index(axis) == root
    return lax.psum(jnp.where(mine, value, jnp.zeros_like(value)), axis)


def solve_right(chol_tile, values):
    return lax.linalg.triangular_solve(
        chol_tile, values, left_side=False, lower=True, transpose_a=True
    )


def keep_mask(tiles, chosen):
    return jnp.all(tiles[:, None] != chosen[None, :], axis=1).astype(jnp.float32)


def outer_product(rows_factor, cols_factor):
    return lax.dot_general(
        rows_factor, cols_factor, (((1,), (0,)), ((), ())), precision=lax.Precision.HIGHEST
    )


def on_device(covariance, panels, observed, drift_basis):
    rows_here = covariance.shape[0]
    cols_here = covariance.shape[1]
    row_start = lax.axis_index("row") * rows_here
    col_start = lax.axis_index("col") * cols_here
    row_tiles = (row_start + lax.iota(jnp.int32, rows_here)) // B
    col_tiles = (col_start + lax.iota(jnp.int32, cols_here)) // B
    sides = jnp.concatenate([observed[None, :], drift_basis], axis=0)
    matrix = covariance
    factors = []
    for position in range(K):
        target = panels[position]
        offset = target * B
        row_owner = offset // rows_here
        col_owner = offset // cols_here
        col_off = offset - col_owner * cols_here
        keep_rows = keep_mask(row_tiles, panels[:position])
        keep_cols = keep_mask(col_tiles, panels[:position])
        col_slab = lax.dynamic_slice_in_dim(matrix, col_off, B, 1)
        col_slab = from_root(col_slab, "col", col_owner)
        side_tile = sides
        diag_tile = col_slab
        row_slab = matrix
        row_slab, diag_tile, side_tile = (
            broadcast(row_slab, "row", row_owner),
            broadcast(diag_tile, "row", row_owner),
            broadcast(side_tile, "row", row_owner),
        )
        chol_tile = jnp.linalg.cholesky(diag_tile)
        rows_factor = solve_right(chol_tile, col_slab) * keep_rows[:, None]
        cols_factor = (
            lax.linalg.triangular_solve(
                chol_tile, row_slab, left_side=True, lower=True, transpose_a=False
            )
            * keep_cols[None, :]
        )
        solved = solve_right(chol_tile, side_tile)
        matrix = matrix - outer_product(rows_factor, cols_factor)
        sides = sides - lax.dot_general(
            solved, rows_factor, (((1,), (1,)), ((), ())), precision=lax.Precision.HIGHEST
        )
        sides = jnp.where((row_tiles == target)[None, :], solved, sides)
        factors.append(rows_factor)
    final_rows = keep_mask(row_tiles, panels)
    final_cols = keep_mask(col_tiles, panels)
    complement = matrix * final_rows[:, None] * final_cols[None, :]
    return (complement, jnp.concatenate(factors, axis=1), sides[0], sides[1:])


def solution(mesh):
    return jax.shard_map(
        on_device,
        mesh=mesh,
        in_specs=(P("row", "col"), P(), P("row"), P(None, "row")),
        out_specs=(P("row", "col"), P("row", None), P("row"), P(None, "row")),
        check_vma=False,
    )
```

profile of v0, /device:TPU:6, one launch (start us, length us, event | category | flops | bytes accessed | tf_op | source)
XLA Modules:
  0.0 943.6 jit_solution(15376847191350219697)
XLA Ops:
  7.2 1.4 fusion.110
  9.3 1.7 constant_dynamic-slice_fusion.11
  11.1 1.5 fusion.62
  12.6 1.1 broadcast_select_fusion.3
  13.6 41.5 %all-gather.9.cloned.1.call-done = f32[2048,256]{1,0:T(8,128)} async-done(((f32[256,256]{1,0:T(8,128)}), f32[2048,256]{1,0:T(8,128)}) %all-gather.9.cloned.1.call-update) | async-done | bytes 2097168 | tf_op jit(solution)/shard_map/all_gather | solution.py:11
  55.2 1.0 constant_dynamic-slice_fusion.10
  57.8 117.0 %all-reduce.16.cloned.1.call-done = (f32[256,1024]{1,0:T(8,128)}, f32[256,256]{0,1:T(8,128)}, f32[65,256]{1,0:T(8,128)}) async-done(((f32[256,1024]{1,0:T(8,128)}, f32[256,256]{0,1:T(8,128)}, f32[65,256]{1,0:T(8,128)}), (f32[256,1024]{1,0:T(8,128)}, f32[256,256]{0,1:T(8,128)}, f32[65,256]{1,0:T(8,128)})) %all-reduce.16.cloned.1.call-update) | async-done | bytes 1377296 | tf_op jit(solution)/shard_map/psum | solution.py:16
  174.8 1.1 copy.18
  175.9 1.0 fusion.29
  176.9 11.7 %cholesky.214 = f32[128,128]{1,0:T(8,128)S(1)} custom-call(f32[128,128]{1,0:T(8,128)S(1)} %cholesky.346), custom_call_target="Cholesky" | custom-call | tf_op jit(solution)/shard_map/jit(cholesky)/cholesky | solution.py:63
  188.6 9.8 %custom-call.29 = f32[1,128,128]{1,2,0:T(8,128)S(1)} custom-call(f32[1,128,128]{2,1,0:T(8,128)S(1)} %get-tuple-element.173), custom_call_target="InvertDiagBlocksLowerTriangular" | custom-call | tf_op jit(solution)/shard_map/jit(cholesky)/cholesky | solution.py:63
  198.9 11.7 %cholesky.231 = f32[128,128]{1,0:T(8,128)S(1)} custom-call(f32[128,128]{1,0:T(8,128)S(1)} %convolution_subtract_fusion.19), custom_call_target="Cholesky" | custom-call | tf_op jit(solution)/shard_map/jit(cholesky)/cholesky | solution.py:63
  212.8 4.2 while.24
  213.6 1.4 bitcast_dynamic-update-slice_fusion.8
  215.6 1.4 bitcast_dynamic-update-slice_fusion.8
  217.0 19.7 %custom-call.30 = f32[2,128,128]{1,2,0:T(8,128)S(1)} custom-call(f32[2,128,128]{2,1,0:T(8,128)S(1)} %get-tuple-element.86), custom_call_target="InvertDiagBlocksLowerTriangular" | custom-call | tf_op jit(solution)/shard_map/triangular_solve/custom-call.0 | solution.py:20
  238.2 1.6 convolution_subtract_fusion.7
  240.5 2.1 broadcast_select_fusion.2
  245.7 37.7 %all-gather.11.cloned.1.call-done = f32[2048,256]{1,0:T(8,128)} async-done(((f32[256,256]{1,0:T(8,128)}), f32[2048,256]{1,0:T(8,128)}) %all-gather.11.cloned.1.call-update) | async-done | bytes 2097168 | tf_op jit(solution)/shard_map/all_gather | solution.py:11
  283.4 1.0 constant_dynamic-slice_fusion.8
  286.2 1.3 compare_convert_fusion.1
  288.2 114.5 %all-reduce.14.cloned.1.call-done = (f32[256,256]{0,1:T(8,128)}, f32[256,1024]{1,0:T(8,128)}, f32[65,256]{1,0:T(8,128)}) async-done(((f32[256,256]{0,1:T(8,128)}, f32[256,1024]{1,0:T(8,128)}, f32[65,256]{1,0:T(8,128)}), (f32[256,256]{0,1:T(8,128)}, f32[256,1024]{1,0:T(8,128)}, f32[65,256]{1,0:T(8,128)})) %all-reduce.14.cloned.1.call-update) | async-done | bytes 1377296 | tf_op jit(solution)/shard_map/psum | solution.py:16
  402.7 1.1 copy.20
  403.8 1.0 fusion.28
  404.8 11.7 %cholesky.248 = f32[128,128]{1,0:T(8,128)S(1)} custom-call(f32[128,128]{1,0:T(8,128)S(1)} %cholesky.349), custom_call_target="Cholesky" | custom-call | tf_op jit(solution)/shard_map/jit(cholesky)/cholesky | solution.py:63
  416.6 9.8 %custom-call.32 = f32[1,128,128]{1,2,0:T(8,128)S(1)} custom-call(f32[1,128,128]{2,1,0:T(8,128)S(1)} %get-tuple-element.169), custom_call_target="InvertDiagBlocksLowerTriangular" | custom-call | tf_op jit(solution)/shard_map/jit(cholesky)/cholesky | solution.py:63
  426.9 11.7 %cholesky.265 = f32[128,128]{1,0:T(8,128)S(1)} custom-call(f32[128,128]{1,0:T(8,128)S(1)} %convolution_subtract_fusion.18), custom_call_target="Cholesky" | custom-call | tf_op jit(solution)/shard_map/jit(cholesky)/cholesky | solution.py:63
  441.3 4.5 while.25
  442.3 1.4 bitcast_dynamic-update-slice_fusion.9
  444.3 1.4 bitcast_dynamic-update-slice_fusion.9
  445.7 19.7 %custom-call.33 = f32[2,128,128]{1,2,0:T(8,128)S(1)} custom-call(f32[2,128,128]{2,1,0:T(8,128)S(1)} %get-tuple-element.88), custom_call_target="InvertDiagBlocksLowerTriangular" | custom-call | tf_op jit(solution)/shard_map/triangular_solve/custom-call.0 | solution.py:20
  466.4 1.7 fusion.19
  468.0 1.6 convolution_subtract_fusion.6
  470.3 2.1 broadcast_select_fusion.1
  474.9 38.3 %all-gather.13.cloned.1.call-done = f32[2048,256]{1,0:T(8,128)} async-done(((f32[256,256]{1,0:T(8,128)}), f32[2048,256]{1,0:T(8,128)}) %all-gather.13.cloned.1.call-update) | async-done | bytes 2097168 | tf_op jit(solution)/shard_map/all_gather | solution.py:11
  513.2 1.0 constant_dynamic-slice_fusion.6
  516.7 115.8 %all-reduce.12.cloned.1.call-done = (f32[256,256]{0,1:T(8,128)}, f32[256,1024]{1,0:T(8,128)}, f32[65,256]{1,0:T(8,128)}) async-done(((f32[256,256]{0,1:T(8,128)}, f32[256,1024]{1,0:T(8,128)}, f32[65,256]{1,0:T(8,128)}), (f32[256,256]{0,1:T(8,128)}, f32[256,1024]{1,0:T(8,128)}, f32[65,256]{1,0:T(8,128)})) %all-reduce.12.cloned.1.call-update) | async-done | bytes 1377296 | tf_op jit(solution)/shard_map/psum | solution.py:16
  632.5 1.1 copy.22
  633.6 1.0 fusion.27
  634.6 11.7 %cholesky.282 = f32[128,128]{1,0:T(8,128)S(1)} custom-call(f32[128,128]{1,0:T(8,128)S(1)} %cholesky.352), custom_call_target="Cholesky" | custom-call | tf_op jit(solution)/shard_map/jit(cholesky)/cholesky | solution.py:63
  646.9 9.8 %custom-call.35 = f32[1,128,128]{1,2,0:T(8,128)S(1)} custom-call(f32[1,128,128]{2,1,0:T(8,128)S(1)} %get-tuple-element.165), custom_call_target="InvertDiagBlocksLowerTriangular" | custom-call | tf_op jit(solution)/shard_map/jit(cholesky)/cholesky | solution.py:63
  657.2 11.7 %cholesky.299 = f32[128,128]{1,0:T(8,128)S(1)} custom-call(f32[128,128]{1,0:T(8,128)S(1)} %convolution_subtract_fusion.17), custom_call_target="Cholesky" | custom-call | tf_op jit(solution)/shard_map/jit(cholesky)/cholesky | solution.py:63
  669.6 1.3 compare_reduce_fusion.9
  672.2 5.6 while.26
  673.7 1.4 bitcast_dynamic-update-slice_fusion.10
  676.4 1.4 bitcast_dynamic-update-slice_fusion.10
  677.8 19.7 %custom-call.36 = f32[2,128,128]{1,2,0:T(8,128)S(1)} custom-call(f32[2,128,128]{2,1,0:T(8,128)S(1)} %get-tuple-element.90), custom_call_target="InvertDiagBlocksLowerTriangular" | custom-call | tf_op jit(solution)/shard_map/triangular_solve/custom-call.0 | solution.py:20
  700.3 2.1 broadcast_select_fusion
  705.5 37.7 %all-gather.15.cloned.1.call-done = f32[2048,256]{1,0:T(8,128)} async-done(((f32[256,256]{1,0:T(8,128)}), f32[2048,256]{1,0:T(8,128)}) %all-gather.15.cloned.1.call-update) | async-done | bytes 2097168 | tf_op jit(solution)/shard_map/all_gather | solution.py:11
  746.0 1.1 broadcast_compare_fusion.2
  747.1 115.5 %all-reduce.10.cloned.1.call-done = (f32[256,256]{0,1:T(8,128)}, f32[256,1024]{1,0:T(8,128)}, f32[65,256]{1,0:T(8,128)}) async-done(((f32[256,256]{0,1:T(8,128)}, f32[256,1024]{1,0:T(8,128)}, f32[65,256]{1,0:T(8,128)}), (f32[256,256]{0,1:T(8,128)}, f32[256,1024]{1,0:T(8,128)}, f32[65,256]{1,0:T(8,128)})) %all-reduce.10.cloned.1.call-update) | async-done | bytes 1377296 | tf_op jit(solution)/shard_map/psum | solution.py:16
  862.7 1.1 copy.24
  863.8 1.0 fusion.26
  864.8 11.7 %cholesky.316 = f32[128,128]{1,0:T(8,128)S(1)} custom-call(f32[128,128]{1,0:T(8,128)S(1)} %cholesky.355), custom_call_target="Cholesky" | custom-call | tf_op jit(solution)/shard_map/jit(cholesky)/cholesky | solution.py:63
  876.6 9.8 %custom-call.38 = f32[1,128,128]{1,2,0:T(8,128)S(1)} custom-call(f32[1,128,128]{2,1,0:T(8,128)S(1)} %get-tuple-element.161), custom_call_target="InvertDiagBlocksLowerTriangular" | custom-call | tf_op jit(solution)/shard_map/jit(cholesky)/cholesky | solution.py:63
  886.9 11.7 %cholesky.333 = f32[128,128]{1,0:T(8,128)S(1)} custom-call(f32[128,128]{1,0:T(8,128)S(1)} %convolution_subtract_fusion.16), custom_call_target="Cholesky" | custom-call | tf_op jit(solution)/shard_map/jit(cholesky)/cholesky | solution.py:63
  901.2 4.3 while.27
  902.1 1.4 bitcast_dynamic-update-slice_fusion.11
  904.1 1.4 bitcast_dynamic-update-slice_fusion.11
  905.5 19.7 %custom-call.39 = f32[2,128,128]{1,2,0:T(8,128)S(1)} custom-call(f32[2,128,128]{2,1,0:T(8,128)S(1)} %get-tuple-element.92), custom_call_target="InvertDiagBlocksLowerTriangular" | custom-call | tf_op jit(solution)/shard_map/triangular_solve/custom-call.0 | solution.py:20
  929.0 1.3 copy.25
  930.3 1.7 fusion.15
  932.0 1.6 convolution_subtract_fusion.4
  934.3 2.1 fusion.1
  (172 shorter events, 39.8 us)
Async XLA Ops:
  7.2 48.0 %all-gather.9.cloned.1.call-start = ((), (), s32[]{:S(2)}) async-start(), calls=%async_computation | async-start | bytes 2359296 | tf_op jit(solution)/shard_map/all_gather | solution.py:11
  11.0 163.8 %all-reduce.16.cloned.1.call-start = ((), (), s32[]{:S(2)}) async-start(), calls=%async_computation.7 | async-start | bytes 2768896 | tf_op jit(solution)/shard_map/psum | solution.py:16
  57.0 226.4 %all-gather.11.cloned.1.call-start = ((), (), s32[]{:S(2)}) async-start(), calls=%async_computation.1 | async-start | bytes 2359296 | tf_op jit(solution)/shard_map/all_gather | solution.py:11
  176.8 60.7 %copy-start.2 = (f32[256,1024]{1,0:T(8,128)S(1)}, f32[256,1024]{1,0:T(8,128)}, u32[]{:S(2)}) copy-start(f32[256,1024]{1,0:T(8,128)} %get-tuple-element.147) | copy-start | bytes 3145732
  237.3 3.3 copy-start
  240.5 3.6 copy-start.7
  240.5 4.3 copy-start.4
  240.5 4.3 copy-start.10
  243.3 159.4 %all-reduce.14.cloned.1.call-start = ((), (), s32[]{:S(2)}) async-start(), calls=%async_computation.6 | async-start | bytes 2768896 | tf_op jit(solution)/shard_map/psum | solution.py:16
  285.3 227.9 %all-gather.13.cloned.1.call-start = ((), (), s32[]{:S(2)}) async-start(), calls=%async_computation.2 | async-start | bytes 2359296 | tf_op jit(solution)/shard_map/all_gather | solution.py:11
  445.7 20.6 %copy-start.13 = (s32[2,2]{1,0:T(2,128)}, s32[2,2]{1,0:T(2,128)S(1)}, u32[]{:S(2)}) copy-start(s32[2,2]{1,0:T(2,128)S(1)} %get-tuple-element.455) | copy-start | bytes 52
  470.3 2.9 copy-start.6
  473.1 42.7 %copy-start.9 = (s32[4]{0:T(128)S(1)}, s32[4]{0:T(128)}, u32[]{:S(2)}) copy-start(s32[4]{0:T(128)} %param.12) | copy-start | bytes 52
  473.1 159.4 %all-reduce.12.cloned.1.call-start = ((), (), s32[]{:S(2)}) async-start(), calls=%async_computation.5 | async-start | bytes 2768896 | tf_op jit(solution)/shard_map/psum | solution.py:16
  515.0 228.2 %all-gather.15.cloned.1.call-start = ((), (), s32[]{:S(2)}) async-start(), calls=%async_computation.3 | async-start | bytes 2359296 | tf_op jit(solution)/shard_map/all_gather | solution.py:11
  634.6 63.8 %copy-start.1 = (f32[256,1024]{1,0:T(8,128)S(1)}, f32[256,1024]{1,0:T(8,128)}, u32[]{:S(2)}) copy-start(f32[256,1024]{1,0:T(8,128)} %get-tuple-element.142) | copy-start | bytes 3145732
  698.1 2.2 copy-start.11
  700.3 3.5 copy-start.5
  700.3 4.2 copy-start.3
  703.1 159.5 %all-reduce.10.cloned.1.call-start = ((), (), s32[]{:S(2)}) async-start(), calls=%async_computation.4 | async-start | bytes 2768896 | tf_op jit(solution)/shard_map/psum | solution.py:16
  745.0 156.2 %copy-start.14 = (s32[2,2]{1,0:T(2,128)S(1)}, s32[2,2]{1,0:T(2,128)}, u32[]{:S(2)}) copy-start(s32[2,2]{1,0:T(2,128)} %get-tuple-element.456) | copy-start | bytes 52
  862.7 62.5 %copy-start.8 = (f32[65,256]{1,0:T(8,128)S(1)}, f32[65,256]{1,0:T(8,128)}, u32[]{:S(2)}) copy-start(f32[65,256]{1,0:T(8,128)} %get-tuple-element.140) | copy-start | bytes 199684
  876.5 50.3 %copy-start.12 = (f32[256]{0:T(256)S(1)}, f32[256]{0:T(256)}, u32[]{:S(2)}) copy-start(f32[256]{0:T(256)} %convert_element_type.60) | copy-start | bytes 3076
Sparse Core Ops, SparseCore 0:
  11.1 44.0 all-gather.8
  59.4 115.3 all-reduce.15
  243.5 39.8 all-gather.10
  287.5 115.1 all-reduce.13
  473.2 39.8 all-gather.12
  517.3 115.1 all-reduce.11
  703.3 39.8 all-gather.14
  747.4 115.1 all-reduce.9
where the time goes:
time: 953 us; the launch traced here: 944 us
  waiting for transfers between devices  618 us (65%)
  other arithmetic  233 us (24%)
  local copies, waits for them, and re-layouts  33.9 us (4%)
  matrix products  32.6 us (3%)
  between operations  23.3 us (2%)
    psum x4, waiting for transfers between devices, broadcast(): return lax.psum(jnp.where(mine, value, jnp.zeros_like(value)), axis)  463 us
    all_gather x4, waiting for transfers between devices, from_root(): lax.all_gather(value, axis)  155 us
    another operation x27, other arithmetic, on_device(): chol_tile = jnp.linalg.cholesky(diag_tile)  139 us
    another operation x9, other arithmetic, solve_right(): lax.linalg.triangular_solve(chol_tile, values, left_side=False, lower=Tru...  78.8 us
  transfers between devices with their start and end apart: 8, of which 8 were waited for; matrix products, arithmetic and copies ran while one was open for 1% of the time, Pallas kernels for 0%

commit v1 on v0

v1 whole, which is shorter than its diff:
```python
import jax
import jax.numpy as jnp
from jax import lax
from jax.sharding import PartitionSpec as P

B = 256
K = 4

HIGH = lax.Precision.HIGHEST


def keep_mask(tiles, chosen):
    return jnp.all(tiles[:, None] != chosen[None, :], axis=1).astype(jnp.float32)


def dot(a, b):
    return lax.dot_general(a, b, (((1,), (0,)), ((), ())), precision=HIGH)


def dot_nt(a, b):
    return lax.dot_general(a, b, (((1,), (1,)), ((), ())), precision=HIGH)


def panel_keep(tiles, panels):
    cols = []
    for p in range(K):
        cols.append(jnp.broadcast_to(keep_mask(tiles, panels[:p])[:, None], (tiles.shape[0], B)))
    return jnp.concatenate(cols, axis=1)


def on_device(covariance, panels, observed, drift_basis):
    rows_here = covariance.shape[0]
    cols_here = covariance.shape[1]
    r = lax.axis_index("row")
    row_start = r * rows_here
    col_start = lax.axis_index("col") * cols_here
    row_tiles = (row_start + lax.iota(jnp.int32, rows_here)) // B
    col_tiles = (col_start + lax.iota(jnp.int32, cols_here)) // B
    sides = jnp.concatenate([observed[None, :], drift_basis], axis=0)

    with jax.named_scope("gather_row_strip"):
        strip = lax.all_gather(covariance, "col", axis=1, tiled=True)
        panel_cols = jnp.concatenate(
            [lax.dynamic_slice_in_dim(strip, panels[j] * B, B, 1) for j in range(K)], axis=1
        )

    with jax.named_scope("share_panel_rows"):
        s_rows, a_rows, w_cols = [], [], []
        for j in range(K):
            off = panels[j] * B - row_start
            mine = (off >= 0) & (off < rows_here)
            off = jnp.clip(off, 0, rows_here - B)
            s_rows.append(jnp.where(mine, lax.dynamic_slice_in_dim(panel_cols, off, B, 0), 0.0))
            a_rows.append(jnp.where(mine, lax.dynamic_slice_in_dim(covariance, off, B, 0), 0.0))
            w_cols.append(jnp.where(mine, lax.dynamic_slice_in_dim(sides, off, B, 1), 0.0))
        rows_buf = jnp.concatenate(
            [jnp.concatenate(s_rows, axis=0), jnp.concatenate(a_rows, axis=0)], axis=1
        )
        w_buf = jnp.concatenate(w_cols, axis=1)
        rows_buf, w_buf = lax.psum((rows_buf, w_buf), "row")
        s_full = rows_buf[:, : K * B]
        a_panel_rows = rows_buf[:, K * B :]

    with jax.named_scope("block_cholesky"):
        chol = jnp.linalg.cholesky(s_full)

    with jax.named_scope("forward_solves"):
        rhs = jnp.concatenate([panel_cols, w_buf], axis=0)
        solved = lax.linalg.triangular_solve(
            chol, rhs, left_side=False, lower=True, transpose_a=True
        )
        factor_rows = solved[:rows_here] * panel_keep(row_tiles, panels)
        z = solved[rows_here:]
        factor_cols_t = lax.linalg.triangular_solve(
            chol, a_panel_rows, left_side=True, lower=True, transpose_a=False
        ) * panel_keep(col_tiles, panels).T

    with jax.named_scope("complement_update"):
        final_rows = keep_mask(row_tiles, panels)
        final_cols = keep_mask(col_tiles, panels)
        complement = (covariance - dot(factor_rows, factor_cols_t)) * final_rows[:, None] * final_cols[None, :]

    with jax.named_scope("sides_update"):
        new_sides = sides - dot_nt(z, factor_rows)
        for j in range(K):
            off = panels[j] * B - row_start
            placed = lax.dynamic_update_slice_in_dim(
                jnp.zeros_like(new_sides), z[:, j * B : (j + 1) * B], jnp.clip(off, 0, rows_here - B), 1
            )
            new_sides = jnp.where((row_tiles == panels[j])[None, :], placed, new_sides)

    return (complement, factor_rows, new_sides[0], new_sides[1:])


def solution(mesh):
    return jax.shard_map(
        on_device,
        mesh=mesh,
        in_specs=(P("row", "col"), P(), P("row"), P(None, "row")),
        out_specs=(P("row", "col"), P("row", None), P("row"), P(None, "row")),
        check_vma=False,
    )
```

time: 953 us -> 688 us (0.72)
  waiting for transfers between devices: 618 us -> 212 us
  matrix products: 32.6 us -> 108 us
  other arithmetic: 233 us -> 285 us
  local copies, waits for them, and re-layouts: 33.9 us -> 52.9 us
    psum x4 -> x1, waiting for transfers between devices: 463 us -> 123 us  [on_device(): rows_buf, w_buf = lax.psum((rows_buf, w_buf), 'row')]
    another operation x44, matrix products: 20.8 us -> 100 us  [the longest x15 51.7 us: on_device(): lax.linalg.triangular_solve(chol, a_panel_rows, left_side=True, lower=Tru...]
    all_gather x4 -> x1, waiting for transfers between devices: 155 us -> 89 us  [on_device(): strip = lax.all_gather(covariance, 'col', axis=1, tiled=True)]
    another operation x36 -> x33, other arithmetic: 218 us -> 256 us  [the longest x30 172 us: on_device(): chol = jnp.linalg.cholesky(s_full)]
    another operation x37 -> x41, local copies, waits for them, and re-layouts: 17.4 us -> 29.6 us  [the longest x29 17.3 us: solve_right(): lax.linalg.triangular_solve(chol_tile, values, left_side=False, lower=Tru...]
    concatenate x1 -> x3, other arithmetic: 0.07 us -> 12.2 us  [the longest x1 10.2 us: on_device(): jnp.concatenate([jnp.concatenate(s_rows, axis=0), jnp.concatenate(a_rows,...]
    slice x3 -> x5, local copies, waits for them, and re-layouts: 2.6 us -> 12.5 us  [the longest x2 10.3 us: on_device(): s_full = rows_buf[:, :K * B]]
  transfers between devices with their start and end apart: 8 -> 2, of which waited for: 8 -> 2; matrix products, arithmetic and copies ran while one was open for 1% -> 2% of each run, Pallas kernels for 0% -> 0%
where the time goes in v1:
time: 688 us; the launch traced here: 681 us
  other arithmetic  285 us (41%)
  waiting for transfers between devices  212 us (31%)
  matrix products  108 us (16%)
  local copies, waits for them, and re-layouts  52.9 us (8%)
  between operations  22.9 us (3%)
    another operation x30, other arithmetic, on_device(): chol = jnp.linalg.cholesky(s_full)  172 us
    psum x1, waiting for transfers between devices, on_device(): rows_buf, w_buf = lax.psum((rows_buf, w_buf), 'row')  123 us
    all_gather x1, waiting for transfers between devices, on_device(): strip = lax.all_gather(covariance, 'col', axis=1, tiled=True)  89 us
    another operation x3, other arithmetic, on_device(): lax.linalg.triangular_solve(chol, rhs, left_side=False, lower=True, trans...  83.9 us
    another operation x15, matrix products, on_device(): lax.linalg.triangular_solve(chol, a_panel_rows, left_side=True, lower=Tru...  51.7 us
    another operation x15, matrix products, on_device(): lax.linalg.triangular_solve(chol, rhs, left_side=False, lower=True, trans...  25.6 us
    another operation x14, matrix products, on_device(): chol = jnp.linalg.cholesky(s_full)  23.1 us
    another operation x24, local copies, waits for them, and re-layouts  22.4 us
  transfers between devices with their start and end apart: 2, of which 2 were waited for; matrix products, arithmetic and copies ran while one was open for 2% of the time, Pallas kernels for 0%

profile of v1, /device:TPU:6, one launch (start us, length us, event | category | flops | bytes accessed | tf_op | source)
XLA Modules:
  0.0 680.6 jit_solution(17626151562019785900)
XLA Ops:
  7.2 2.5 copy.43
  18.5 89.0 %all-gather.2.cloned.1.call-done = f32[256,8192]{0,1:T(8,128)} async-done(((f32[256,1024]{0,1:T(8,128)}), f32[256,8192]{0,1:T(8,128)}) %all-gather.2.cloned.1.call-update) | async-done | bytes 8388624 | tf_op jit(solution)/shard_map/gather_row_strip/all_gather | solution.py:42
  109.7 10.2 %maximum_maximum_fusion = f32[1024,2048]{0,1:T(8,128)} fusion(f32[256,1024]{0,1:T(8,128)S(1)} %get-tuple-element.46, f32[256,1024]{0,1:T(8,128)S(1)} %copy-done.4, f32[256,1024]{0,1:T(8,128)S(1)} %copy-done.5, f32[256,1024]{0,1:T(8,128)S(1)} %get-tuple-element.45, f32[256,1024]{0,1:T(8,128)S(1)} %broadcast_select_fusion.4, ...), kind=kLoop, calls=%fused_computation.2 | loop fusion | flops 14680064 | bytes 16777216 | tf_op jit(solution)/shard_map/share_panel_rows/concatenate | solution.py:56
  124.1 1.9 broadcast_compare_fusion.1
  126.0 1.9 compare_convert_fusion.1
  129.1 122.7 %all-reduce.4.cloned.1.call-done = (f32[65,1024]{0,1:T(8,128)}, f32[1024,2048]{0,1:T(8,128)}) async-done(((f32[65,1024]{0,1:T(8,128)}, f32[1024,2048]{0,1:T(8,128)}), (f32[65,1024]{0,1:T(8,128)}, f32[1024,2048]{0,1:T(8,128)})) %all-reduce.4.cloned.1.call-update) | async-done | bytes 8654864 | tf_op jit(solution)/shard_map/share_panel_rows/psum | solution.py:60
  251.9 4.7 slice.373
  256.6 5.5 copy.50
  262.1 4.4 fusion.8
  266.6 2.0 copy-done
  268.6 11.7 %cholesky.223 = f32[128,128]{1,0:T(8,128)S(1)} custom-call(f32[128,128]{1,0:T(8,128)S(1)} %cholesky.580), custom_call_target="Cholesky" | custom-call | tf_op jit(solution)/shard_map/block_cholesky/jit(cholesky)/cholesky | solution.py:65
  280.3 2.5 cholesky.255
  282.8 9.8 %custom-call.64 = f32[1,128,128]{1,2,0:T(8,128)S(1)} custom-call(f32[1,128,128]{2,1,0:T(8,128)S(1)} %get-tuple-element.123), custom_call_target="InvertDiagBlocksLowerTriangular" | custom-call | tf_op jit(solution)/shard_map/block_cholesky/jit(cholesky)/cholesky | solution.py:65
  292.6 2.4 constant_dynamic-update-slice_fusion.51
  296.5 11.9 %cholesky.244 = f32[128,128]{1,0:T(8,128)S(1)} custom-call(f32[128,128]{1,0:T(8,128)S(1)} %cholesky.584), custom_call_target="Cholesky" | custom-call | tf_op jit(solution)/shard_map/block_cholesky/jit(cholesky)/cholesky | solution.py:65
  309.1 9.8 %custom-call.65 = f32[1,128,128]{1,2,0:T(8,128)S(1)} custom-call(f32[1,128,128]{2,1,0:T(8,128)S(1)} %get-tuple-element.120), custom_call_target="InvertDiagBlocksLowerTriangular" | custom-call | tf_op jit(solution)/shard_map/block_cholesky/jit(cholesky)/cholesky | solution.py:65
  320.2 2.1 convolution_subtract_fusion.6
  322.3 11.7 %cholesky.468 = f32[128,128]{1,0:T(8,128)S(1)} custom-call(f32[128,128]{1,0:T(8,128)S(1)} %cholesky.589), custom_call_target="Cholesky" | custom-call | tf_op jit(solution)/shard_map/block_cholesky/jit(cholesky)/cholesky | solution.py:65
  335.3 9.8 %custom-call.66 = f32[1,128,128]{1,2,0:T(8,128)S(1)} custom-call(f32[1,128,128]{2,1,0:T(8,128)S(1)} %get-tuple-element.117), custom_call_target="InvertDiagBlocksLowerTriangular" | custom-call | tf_op jit(solution)/shard_map/block_cholesky/jit(cholesky)/cholesky | solution.py:65
  346.3 2.3 convolution_subtract_fusion.7
  348.6 12.1 %cholesky.487 = f32[128,128]{1,0:T(8,128)S(1)} custom-call(f32[128,128]{1,0:T(8,128)S(1)} %cholesky.594), custom_call_target="Cholesky" | custom-call | tf_op jit(solution)/shard_map/block_cholesky/jit(cholesky)/cholesky | solution.py:65
  362.1 9.8 %custom-call.67 = f32[1,128,128]{1,2,0:T(8,128)S(1)} custom-call(f32[1,128,128]{2,1,0:T(8,128)S(1)} %get-tuple-element.114), custom_call_target="InvertDiagBlocksLowerTriangular" | custom-call | tf_op jit(solution)/shard_map/block_cholesky/jit(cholesky)/cholesky | solution.py:65
  373.0 2.3 convolution_subtract_fusion.8
  375.3 11.7 %cholesky.506 = f32[128,128]{1,0:T(8,128)S(1)} custom-call(f32[128,128]{1,0:T(8,128)S(1)} %cholesky.599), custom_call_target="Cholesky" | custom-call | tf_op jit(solution)/shard_map/block_cholesky/jit(cholesky)/cholesky | solution.py:65
  388.4 9.9 %custom-call.68 = f32[1,128,128]{1,2,0:T(8,128)S(1)} custom-call(f32[1,128,128]{2,1,0:T(8,128)S(1)} %get-tuple-element.111), custom_call_target="InvertDiagBlocksLowerTriangular" | custom-call | tf_op jit(solution)/shard_map/block_cholesky/jit(cholesky)/cholesky | solution.py:65
  399.4 2.3 convolution_subtract_fusion.16
  401.7 11.7 %cholesky.526 = f32[128,128]{1,0:T(8,128)S(1)} custom-call(f32[128,128]{1,0:T(8,128)S(1)} %cholesky.604), custom_call_target="Cholesky" | custom-call | tf_op jit(solution)/shard_map/block_cholesky/jit(cholesky)/cholesky | solution.py:65
  414.8 9.8 %custom-call.69 = f32[1,128,128]{1,2,0:T(8,128)S(1)} custom-call(f32[1,128,128]{2,1,0:T(8,128)S(1)} %get-tuple-element.108), custom_call_target="InvertDiagBlocksLowerTriangular" | custom-call | tf_op jit(solution)/shard_map/block_cholesky/jit(cholesky)/cholesky | solution.py:65
  425.5 2.0 convolution_subtract_fusion.17
  427.6 11.9 %cholesky.546 = f32[128,128]{1,0:T(8,128)S(1)} custom-call(f32[128,128]{1,0:T(8,128)S(1)} %cholesky.609), custom_call_target="Cholesky" | custom-call | tf_op jit(solution)/shard_map/block_cholesky/jit(cholesky)/cholesky | solution.py:65
  440.8 9.8 %custom-call.70 = f32[1,128,128]{1,2,0:T(8,128)S(1)} custom-call(f32[1,128,128]{2,1,0:T(8,128)S(1)} %get-tuple-element.105), custom_call_target="InvertDiagBlocksLowerTriangular" | custom-call | tf_op jit(solution)/shard_map/block_cholesky/jit(cholesky)/cholesky | solution.py:65
  451.4 1.8 convolution_subtract_fusion.19
  453.2 11.7 %cholesky.564 = f32[128,128]{1,0:T(8,128)S(1)} custom-call(f32[128,128]{1,0:T(8,128)S(1)} %convolution_subtract_fusion.19), custom_call_target="Cholesky" | custom-call | tf_op jit(solution)/shard_map/block_cholesky/jit(cholesky)/cholesky | solution.py:65
  471.9 4.9 select_select_fusion
  476.8 22.5 %while.1 = (s32[]{:T(128)}, f32[1024,1024]{1,0:T(8,128)}, s32[8,2]{0,1:T(2,128)S(1)}, f32[8,128,128]{2,1,0:T(8,128)S(1)}, s32[]{:T(128)}) while((s32[]{:T(128)}, f32[1024,1024]{1,0:T(8,128)}, s32[8,2]{0,1:T(2,128)S(1)}, f32[8,128,128]{2,1,0:T(8,128)S(1)}, s32[]{:T(128)}) %tuple.106), condition=%wide.while_cond, body=%wide.while_body.sunk | while | flops 2 | bytes 131181 | solution.py:69
  477.4 2.2 bitcast_dynamic-update-slice_fusion.2
  480.2 2.2 bitcast_dynamic-update-slice_fusion.2
  483.1 2.2 bitcast_dynamic-update-slice_fusion.2
  485.9 2.2 bitcast_dynamic-update-slice_fusion.2
  488.7 2.2 bitcast_dynamic-update-slice_fusion.2
  491.5 2.2 bitcast_dynamic-update-slice_fusion.2
  494.4 2.2 bitcast_dynamic-update-slice_fusion.2
  497.2 2.1 bitcast_dynamic-update-slice_fusion.2
  499.4 79.0 %custom-call.71 = f32[8,128,128]{1,2,0:T(8,128)S(1)} custom-call(f32[8,128,128]{2,1,0:T(8,128)S(1)} %get-tuple-element.11), custom_call_target="InvertDiagBlocksLowerTriangular" | custom-call | tf_op jit(solution)/shard_map/forward_solves/triangular_solve | solution.py:69
  590.0 2.5 convolution_subtract_fusion.11
  595.1 2.3 constant_dynamic-update-slice_fusion.13
  597.4 2.3 convolution_subtract_fusion.15
  601.0 2.5 convolution_subtract_fusion.10
  604.8 2.7 convolution_subtract_fusion.9
  612.3 2.4 fusion.42
  615.5 3.2 constant_dynamic-update-slice_fusion.43
  619.4 2.2 convolution_subtract_fusion.4
  621.7 2.1 constant_dynamic-update-slice_fusion.42
  623.8 2.9 convolution_subtract_fusion
  626.8 2.1 constant_dynamic-update-slice_fusion.41
  628.9 3.8 fusion.33
  632.7 2.1 constant_dynamic-update-slice_fusion.40
  634.9 4.6 fusion.36
  639.5 2.2 constant_dynamic-update-slice_fusion.39
  641.6 6.4 convolution_subtract_fusion.2
  648.1 1.9 constant_dynamic-update-slice_fusion.38
  650.0 7.3 %convolution_subtract_fusion.1 = f32[128,1024]{0,1:T(8,128)S(1)} fusion(f32[768,1024]{1,0:T(8,128)} %get-tuple-element.53, f32[1024,2048]{0,1:T(8,128)} %get-tuple-element.33, f32[1024,1024]{1,0:T(8,128)} %get-tuple-element.202), kind=kOutput, calls=%fused_computation.37 | convolution fusion | flops 1208090624 | bytes 4587520 | tf_op jit(solution)/shard_map/forward_solves/triangular_solve | solution.py:74
  658.8 8.5 %convolution_subtract_fusion.3 = f32[128,1024]{0,1:T(8,128)S(1)} fusion(f32[896,1024]{1,0:T(8,128)} %get-tuple-element.49, f32[1024,2048]{0,1:T(8,128)} %get-tuple-element.33, f32[1024,1024]{1,0:T(8,128)} %get-tuple-element.202), kind=kOutput, calls=%fused_computation.41 | convolution fusion | flops 1409417216 | bytes 5177344 | tf_op jit(solution)/shard_map/forward_solves/triangular_solve | solution.py:74
  668.4 5.0 fusion.30
  (158 shorter events, 61.1 us)
Async XLA Ops:
  7.2 100.3 %all-gather.2.cloned.1.call-start = ((), (), s32[]{:S(2)}) async-start(), calls=%async_computation | async-start | bytes 9437184 | tf_op jit(solution)/shard_map/gather_row_strip/all_gather | solution.py:42
  9.7 7.0 %copy-start.1 = (f32[256,1024]{0,1:T(8,128)S(1)}, f32[256,1024]{0,1:T(8,128)}, u32[]{:S(2)}) copy-start(f32[256,1024]{0,1:T(8,128)} %copy.43) | copy-start | bytes 3145732
  9.8 242.1 %all-reduce.4.cloned.1.call-start = ((), (), s32[]{:S(2)}) async-start(), calls=%async_computation.1 | async-start | bytes 17825792 | tf_op jit(solution)/shard_map/share_panel_rows/psum | solution.py:60
  18.5 91.2 %copy-start.4 = (f32[256,1024]{0,1:T(8,128)S(1)}, f32[256,1024]{0,1:T(8,128)}, u32[]{:S(2)}) copy-start(f32[256,1024]{0,1:T(8,128)} %get-tuple-element.47) | copy-start | bytes 3145732
  107.4 2.2 copy-start.5
  108.8 0.7 copy-start.6
  108.8 0.8 copy-start.8
  108.8 0.9 copy-start.10
  119.9 0.7 copy-start.14
  266.6 2.0 copy-start
  471.9 106.5 %copy-start.7 = (f32[256,256]{0,1:T(8,128)S(1)}, f32[256,256]{0,1:T(8,128)}, u32[]{:S(2)}) copy-start(f32[256,256]{0,1:T(8,128)} %copy-done.6) | copy-start | bytes 786436
  471.9 106.5 %copy-start.9 = (f32[256,256]{0,1:T(8,128)S(1)}, f32[256,256]{0,1:T(8,128)}, u32[]{:S(2)}) copy-start(f32[256,256]{0,1:T(8,128)} %copy-done.8) | copy-start | bytes 786436
  471.9 106.5 %copy-start.11 = (f32[256,256]{0,1:T(8,128)S(1)}, f32[256,256]{0,1:T(8,128)}, u32[]{:S(2)}) copy-start(f32[256,256]{0,1:T(8,128)} %copy-done.10) | copy-start | bytes 786436
  589.4 0.7 copy-start.13
  597.4 13.2 %copy-start.16 = (f32[256]{0:T(256)S(1)}, f32[256]{0:T(256)}, u32[]{:S(2)}) copy-start(f32[256]{0:T(256)} %get-tuple-element.143) | copy-start | bytes 3076
  599.6 11.1 %copy-start.21 = (f32[256]{0:T(256)S(1)}, f32[256]{0:T(256)}, u32[]{:S(2)}) copy-start(f32[256]{0:T(256)} %convert_element_type.57) | copy-start | bytes 3076
  599.6 11.2 %copy-start.22 = (f32[256]{0:T(256)S(1)}, f32[256]{0:T(256)}, u32[]{:S(2)}) copy-start(f32[256]{0:T(256)} %convert_element_type.58) | copy-start | bytes 3076
  603.5 8.9 %copy-start.17 = (pred[256]{0:T(512)(128)(4,1)S(1)}, pred[256]{0:T(512)(128)(4,1)}, u32[]{:S(2)}) copy-start(pred[256]{0:T(512)(128)(4,1)} %get-tuple-element.145) | copy-start | bytes 772
  603.5 8.9 %copy-start.18 = (pred[256]{0:T(512)(128)(4,1)S(1)}, pred[256]{0:T(512)(128)(4,1)}, u32[]{:S(2)}) copy-start(pred[256]{0:T(512)(128)(4,1)} %get-tuple-element.146) | copy-start | bytes 772
  603.5 8.9 %copy-start.19 = (pred[256]{0:T(512)(128)(4,1)S(1)}, pred[256]{0:T(512)(128)(4,1)}, u32[]{:S(2)}) copy-start(pred[256]{0:T(512)(128)(4,1)} %get-tuple-element.144) | copy-start | bytes 772
  603.5 8.9 %copy-start.23 = (pred[256]{0:T(512)(128)(4,1)S(1)}, pred[256]{0:T(512)(128)(4,1)}, u32[]{:S(2)}) copy-start(pred[256]{0:T(512)(128)(4,1)} %broadcast_compare_fusion.3) | copy-start | bytes 772
  612.3 56.0 %copy-start.2 = (f32[256,1024]{1,0:T(8,128)}, f32[256,1024]{1,0:T(8,128)S(1)}, u32[]{:S(2)}) copy-start(f32[256,1024]{1,0:T(8,128)S(1)} %slice_multiply_fusion) | copy-start | bytes 3145732
  650.0 7.3 %copy-start.3 = (f32[1024,1024]{1,0:T(8,128)S(1)}, f32[1024,1024]{1,0:T(8,128)}, u32[]{:S(2)}) copy-start(f32[1024,1024]{1,0:T(8,128)} %get-tuple-element.52) | copy-start | bytes 12582916
  657.3 10.7 %copy-start.15 = (f32[1024]{0:T(1024)S(1)}, f32[1024]{0:T(1024)}, u32[]{:S(2)}) copy-start(f32[1024]{0:T(1024)} %compare_convert_fusion) | copy-start | bytes 12292
  658.8 9.6 %copy-start.12 = (f32[256,1024]{1,0:T(8,128)S(1)}, f32[256,1024]{1,0:T(8,128)}, u32[]{:S(2)}) copy-start(f32[256,1024]{1,0:T(8,128)} %param.4) | copy-start | bytes 3145732
  658.8 9.6 %copy-start.20 = (f32[256]{0:T(256)S(1)}, f32[256]{0:T(256)}, u32[]{:S(2)}) copy-start(f32[256]{0:T(256)} %convert_element_type.62) | copy-start | bytes 3076
Sparse Core Ops, SparseCore 0:
  10.4 97.0 all-gather.1
  120.1 131.7 all-reduce.3

commit v2 on v1

--- a/solution.py
+++ b/solution.py
@@ -2,6 +2,8 @@
 import jax.numpy as jnp
 from jax import lax
 from jax.sharding import PartitionSpec as P
+from jax.experimental import pallas as pl
+from jax.experimental.pallas import tpu as pltpu
 
 B = 256
 K = 4
@@ -19,6 +21,53 @@
 
 def dot_nt(a, b):
     return lax.dot_general(a, b, (((1,), (1,)), ((), ())), precision=HIGH)
+
+
+NB = 128
+
+
+def chol_inv_kernel(d_ref, out_ref):
+    n = d_ref.shape[0]
+    rows = lax.broadcasted_iota(jnp.int32, (n, n), 0)
+    cols = lax.broadcasted_iota(jnp.int32, (n, n), 1)
+    out_ref[:n, :] = d_ref[...]
+    out_ref[n:, :] = (rows == cols).astype(jnp.float32)
+    lane = lax.broadcasted_iota(jnp.int32, (1, n), 1)
+    row2 = lax.broadcasted_iota(jnp.int32, (2 * n, 1), 0)
+    for k in range(n):
+        m = out_ref[...]
+        rowk = out_ref[k : k + 1, :]
+        s = lax.rsqrt(rowk[:, k : k + 1])
+        col = jnp.where(row2 >= k, m[:, k : k + 1] * s, 0.0)
+        rowv = jnp.where(lane > k, rowk * s, 0.0)
+        m = jnp.where(lane == k, col, m - col * rowv)
+        out_ref[...] = m
+
+
+def chol_inv(d):
+    n = d.shape[0]
+    return pl.pallas_call(
+        chol_inv_kernel,
+        out_shape=jax.ShapeDtypeStruct((2 * n, n), jnp.float32),
+        in_specs=[pl.BlockSpec(memory_space=pltpu.VMEM)],
+        out_specs=pl.BlockSpec(memory_space=pltpu.VMEM),
+        cost_estimate=pl.CostEstimate(flops=6 * n * n * n, bytes_accessed=12 * n * n, transcendentals=n),
+    )(d)
+
+
+def blocked_solve(s_mat, rhs):
+    n = s_mat.shape[0]
+    solved = []
+    for a in range(0, n, NB):
+        out = chol_inv(s_mat[:NB, :NB])
+        inv_t = out[NB:]
+        p_rhs = dot(rhs[:, :NB], inv_t)
+        solved.append(p_rhs)
+        if a + NB < n:
+            p_s = dot(s_mat[NB:, :NB], inv_t)
+            s_mat = s_mat[NB:, NB:] - dot_nt(p_s, p_s)
+            rhs = rhs[:, NB:] - dot_nt(p_rhs, p_s)
+    return jnp.concatenate(solved, axis=1)
 
 
 def panel_keep(tiles, panels):
@@ -61,24 +110,17 @@
         s_full = rows_buf[:, : K * B]
         a_panel_rows = rows_buf[:, K * B :]
 
-    with jax.named_scope("block_cholesky"):
-        chol = jnp.linalg.cholesky(s_full)
-
-    with jax.named_scope("forward_solves"):
-        rhs = jnp.concatenate([panel_cols, w_buf], axis=0)
-        solved = lax.linalg.triangular_solve(
-            chol, rhs, left_side=False, lower=True, transpose_a=True
-        )
+    with jax.named_scope("blocked_cholesky_solve"):
+        rhs = jnp.concatenate([panel_cols, w_buf, a_panel_rows.T], axis=0)
+        solved = blocked_solve(s_full, rhs)
         factor_rows = solved[:rows_here] * panel_keep(row_tiles, panels)
-        z = solved[rows_here:]
-        factor_cols_t = lax.linalg.triangular_solve(
-            chol, a_panel_rows, left_side=True, lower=True, transpose_a=False
-        ) * panel_keep(col_tiles, panels).T
+        z = solved[rows_here : rows_here + w_buf.shape[0]]
+        factor_cols = solved[rows_here + w_buf.shape[0] :] * panel_keep(col_tiles, panels)
 
     with jax.named_scope("complement_update"):
         final_rows = keep_mask(row_tiles, panels)
         final_cols = keep_mask(col_tiles, panels)
-        complement = (covariance - dot(factor_rows, factor_cols_t)) * final_rows[:, None] * final_cols[None, :]
+        complement = (covariance - dot_nt(factor_rows, factor_cols)) * final_rows[:, None] * final_cols[None, :]
 
     with jax.named_scope("sides_update"):
         new_sides = sides - dot_nt(z, factor_rows)

time: 688 us -> 488 us (0.71)
  other arithmetic: 285 us -> 23.7 us
  Pallas kernels: 0 us -> 101 us
  matrix products: 108 us -> 74.2 us
    another operation x33 -> x0, other arithmetic: 256 us -> none  [the longest x30 172 us: on_device(): chol = jnp.linalg.cholesky(s_full)]
    pallas_call x0 -> x8, Pallas kernels: none -> 101 us  [chol_inv(): pl.pallas_call(chol_inv_kernel, out_shape=jax.ShapeDtypeStruct((2 * n, n)...]
    another operation x44 -> x0, matrix products: 100 us -> none  [the longest x15 51.7 us: on_device(): lax.linalg.triangular_solve(chol, a_panel_rows, left_side=True, lower=Tru...]
    dot_general x1 -> x16, matrix products: 2.35 us -> 44.8 us  [dot_nt(): return lax.dot_general(a, b, (((1,), (1,)), ((), ())), precision=HIGH)]
    another operation x41 -> x0, local copies, waits for them, and re-layouts: 29.6 us -> none
    dot_general x1 -> x15, matrix products: 4.99 us -> 29.4 us  [dot(): return lax.dot_general(a, b, (((1,), (0,)), ((), ())), precision=HIGH)]
    concatenate x0 -> x2, local copies, waits for them, and re-layouts: none -> 16.3 us  [the longest x1 9.39 us: on_device(): jnp.concatenate([jnp.concatenate(s_rows, axis=0), jnp.concatenate(a_rows,...]
    dot_general x0 -> x8, local copies, waits for them, and re-layouts: none -> 12.5 us  [dot(): return lax.dot_general(a, b, (((1,), (0,)), ((), ())), precision=HIGH)]
  transfers between devices with their start and end apart: 2 -> 2, of which waited for: 2 -> 2; matrix products, arithmetic and copies ran while one was open for 2% -> 3% of each run, Pallas kernels for 0% -> 0%
where the time goes in v2:
time: 488 us; the launch traced here: 481 us
  waiting for transfers between devices  211 us (43%)
  Pallas kernels  101 us (21%)
  matrix products  74.2 us (15%)
  local copies, waits for them, and re-layouts  53.6 us (11%)
  other arithmetic  23.7 us (5%)
  between operations  17.7 us (4%)
    psum x1, waiting for transfers between devices, on_device(): rows_buf, w_buf = lax.psum((rows_buf, w_buf), 'row')  124 us
    pallas_call x8, Pallas kernels, chol_inv(): pl.pallas_call(chol_inv_kernel, out_shape=jax.ShapeDtypeStruct((2 * n, n)...  101 us
    all_gather x1, waiting for transfers between devices, on_device(): strip = lax.all_gather(covariance, 'col', axis=1, tiled=True)  87.6 us
    dot_general x16, matrix products, dot_nt(): return lax.dot_general(a, b, (((1,), (1,)), ((), ())), precision=HIGH)  44.8 us
    dot_general x15, matrix products, dot(): return lax.dot_general(a, b, (((1,), (0,)), ((), ())), precision=HIGH)  29.4 us
    dot_general x8, local copies, waits for them, and re-layouts, dot(): return lax.dot_general(a, b, (((1,), (0,)), ((), ())), precision=HIGH)  12.5 us
    concatenate x1, other arithmetic, on_device(): jnp.concatenate([jnp.concatenate(s_rows, axis=0), jnp.concatenate(a_rows,...  10.3 us
  transfers between devices with their start and end apart: 2, of which 2 were waited for; matrix products, arithmetic and copies ran while one was open for 3% of the time, Pallas kernels for 0%

profile of v2, /device:TPU:6, one launch (start us, length us, event | category | flops | bytes accessed | tf_op | source)
XLA Modules:
  0.0 481.5 jit_solution(16109467823129383219)
XLA Ops:
  7.2 2.5 copy.55
  9.8 1.5 fusion.64
  14.7 0.9 copy.57
  17.3 2.5 broadcast_select_fusion.3
  19.9 87.6 %all-gather.2.cloned.1.call-done = f32[256,8192]{0,1:T(8,128)} async-done(((f32[256,1024]{0,1:T(8,128)}), f32[256,8192]{0,1:T(8,128)}) %all-gather.2.cloned.1.call-update) | async-done | bytes 8388624 | tf_op jit(solution)/shard_map/gather_row_strip/all_gather | solution.py:91
  107.4 1.3 constant_dynamic-slice_fusion.3
  108.8 1.2 broadcast_select_fusion.7
  110.1 10.3 %maximum_maximum_fusion = f32[1024,2048]{0,1:T(8,128)} fusion(f32[256,1024]{0,1:T(8,128)S(1)} %get-tuple-element.29, f32[256,1024]{0,1:T(8,128)S(1)} %get-tuple-element.30, f32[256,1024]{0,1:T(8,128)S(1)} %copy-done.9, f32[256,1024]{0,1:T(8,128)S(1)} %get-tuple-element.28, f32[256,1024]{0,1:T(8,128)S(1)} %broadcast_select_fusion.4, ...), kind=kLoop, calls=%fused_computation | loop fusion | flops 14680064 | bytes 16777216 | tf_op jit(solution)/shard_map/share_panel_rows/concatenate | solution.py:105
  120.4 9.4 %copy.62 = f32[1024,2048]{1,0:T(8,128)} copy(f32[1024,2048]{0,1:T(8,128)} %maximum_maximum_fusion) | data formatting | bytes 16777216 | tf_op jit(solution)/shard_map/share_panel_rows/concatenate | solution.py:105
  132.8 1.3 broadcast_compare_fusion.2
  134.1 1.8 broadcast_compare_fusion
  135.9 1.2 compare_convert_fusion.1
  137.7 123.7 %all-reduce.3.cloned.1.call-done = (f32[65,1024]{0,1:T(8,128)}, f32[1024,2048]{1,0:T(8,128)}) async-done(((f32[65,1024]{0,1:T(8,128)}, f32[1024,2048]{1,0:T(8,128)}), (f32[65,1024]{0,1:T(8,128)}, f32[1024,2048]{1,0:T(8,128)})) %all-reduce.3.cloned.1.call-update) | async-done | bytes 8654864 | tf_op jit(solution)/shard_map/share_panel_rows/psum | solution.py:109
  261.5 1.5 slice.266.d_ref
  262.9 4.8 slice_bitcast_fusion
  267.7 12.5 %blocked_cholesky_solve.8 = f32[256,128]{1,0:T(8,128)} custom-call(f32[128,128]{1,0:T(8,128)} %slice.266.d_ref), custom_call_target="tpu_custom_call" | custom-call | flops 12582912 | bytes 196608 | tf_op jit(solution)/shard_map/blocked_cholesky_solve/pallas_call | solution.py:49
  280.2 1.5 fusion.29
  282.6 4.6 slice_subtract_fusion.2
  287.8 12.9 %blocked_cholesky_solve.9 = f32[256,128]{1,0:T(8,128)} custom-call(f32[128,128]{1,0:T(8,128)} %slice.272.d_ref), custom_call_target="tpu_custom_call" | custom-call | flops 12582912 | bytes 196608 | tf_op jit(solution)/shard_map/blocked_cholesky_solve/pallas_call | solution.py:49
  300.7 1.3 fusion.31
  302.1 2.0 slice_subtract_fusion.3
  304.1 1.4 copy-done
  306.1 12.5 %blocked_cholesky_solve.10 = f32[256,128]{1,0:T(8,128)} custom-call(f32[128,128]{1,0:T(8,128)} %slice.278.d_ref), custom_call_target="tpu_custom_call" | custom-call | flops 12582912 | bytes 196608 | tf_op jit(solution)/shard_map/blocked_cholesky_solve/pallas_call | solution.py:49
  318.6 1.4 fusion.33
  320.7 3.1 slice_subtract_fusion.4
  324.5 12.5 %blocked_cholesky_solve.11 = f32[256,128]{1,0:T(8,128)} custom-call(f32[128,128]{1,0:T(8,128)} %slice.284.d_ref), custom_call_target="tpu_custom_call" | custom-call | flops 12582912 | bytes 196608 | tf_op jit(solution)/shard_map/blocked_cholesky_solve/pallas_call | solution.py:49
  337.0 1.2 fusion.36
  338.2 1.0 convolution_subtract_fusion.5
  339.2 1.0 copy-done.14
  340.8 12.5 %blocked_cholesky_solve.12 = f32[256,128]{1,0:T(8,128)} custom-call(f32[128,128]{1,0:T(8,128)} %slice.290.d_ref), custom_call_target="tpu_custom_call" | custom-call | flops 12582912 | bytes 196608 | tf_op jit(solution)/shard_map/blocked_cholesky_solve/pallas_call | solution.py:49
  353.3 1.7 fusion.38
  355.0 1.7 convolution_subtract_fusion.6
  357.4 12.5 %blocked_cholesky_solve.13 = f32[256,128]{1,0:T(8,128)} custom-call(f32[128,128]{1,0:T(8,128)} %slice.296.d_ref), custom_call_target="tpu_custom_call" | custom-call | flops 12582912 | bytes 196608 | tf_op jit(solution)/shard_map/blocked_cholesky_solve/pallas_call | solution.py:49
  369.9 1.1 fusion.40
  372.0 12.5 %blocked_cholesky_solve.14 = f32[256,128]{1,0:T(8,128)} custom-call(f32[128,128]{1,0:T(8,128)} %slice.302.d_ref), custom_call_target="tpu_custom_call" | custom-call | flops 12582912 | bytes 196608 | tf_op jit(solution)/shard_map/blocked_cholesky_solve/pallas_call | solution.py:49
  384.5 1.0 fusion.44
  386.5 6.9 %concatenate.48 = f32[1345,1024]{0,1:T(8,128)} concatenate(f32[256,1024]{0,1:T(8,128)S(1)} %copy-done.13, f32[65,1024]{0,1:T(8,128)S(1)} %copy-done.21, f32[1024,1024]{0,1:T(8,128)} %slice_bitcast_fusion), dimensions={0} | concatenate | bytes 11018240 | tf_op jit(solution)/shard_map/blocked_cholesky_solve/concatenate | solution.py:114
  393.4 3.3 constant_dynamic-update-slice_fusion.7
  396.8 6.5 %slice_subtract_fusion = f32[1345,896]{0,1:T(8,128)S(1)} fusion(f32[1345,1024]{0,1:T(8,128)} %concatenate.48, f32[1345,128]{1,0:T(8,128)S(1)} %get-tuple-element.40, f32[896,128]{1,0:T(8,128)S(1)} %copy-done.2), kind=kOutput, calls=%fused_computation.1 | convolution fusion | flops 1852269440 | bytes 10788352 | tf_op jit(solution)/shard_map/blocked_cholesky_solve/dot_general | solution.py:23
  403.3 2.3 constant_dynamic-update-slice_fusion.6
  405.5 3.8 slice_subtract_fusion.1
  409.3 2.3 constant_dynamic-update-slice_fusion.5
  411.6 3.2 convolution_subtract_fusion
  414.9 2.2 constant_dynamic-update-slice_fusion.4
  417.1 2.7 convolution_subtract_fusion.1
  419.9 2.2 constant_dynamic-update-slice_fusion.3
  422.1 1.9 convolution_subtract_fusion.2
  424.1 2.3 constant_dynamic-update-slice_fusion.2
  426.3 1.3 convolution_subtract_fusion.3
  427.7 2.3 constant_dynamic-update-slice_fusion.1
  430.0 1.7 convolution_subtract_fusion.4
  431.6 1.1 copy.70
  432.8 1.2 copy.73
  433.9 2.3 copy.72
  436.2 2.3 copy.75
  438.5 1.1 copy.74
  439.6 1.1 copy.77
  440.8 1.1 copy.76
  441.9 12.8 %blocked_cholesky_solve.15 = f32[256,128]{1,0:T(8,128)} custom-call(f32[128,128]{1,0:T(8,128)} %convolution_subtract_fusion.9.d_ref), custom_call_target="tpu_custom_call" | custom-call | flops 12582912 | bytes 196608 | tf_op jit(solution)/shard_map/blocked_cholesky_solve/pallas_call | solution.py:49
  454.7 3.3 constant_dynamic-update-slice_fusion
  458.0 2.3 copy.71
  460.6 1.4 slice_multiply_fusion.8
  462.1 2.3 fusion.14
  466.6 7.6 %fusion.10 = f32[256,1024]{1,0:T(8,128)} fusion(f32[256,1024]{1,0:T(8,128)} %param.4, f32[256,1024]{1,0:T(8,128)S(1)} %slice_multiply_fusion.8, f32[1345,1024]{1,0:T(8,128)} %get-tuple-element.53, f32[1024,256]{1,0:T(8,128)S(1)} %broadcast_in_dim.118, f32[1024,256]{1,0:T(8,128)S(1)} %broadcast_in_dim.117, f32[1024,256]{1,0:T(8,128)S(1)} %broadcast_in_dim.116, ...), kind=kOutput, calls=%fused_computation.24 | convolution fusion | flops 3226206208 | bytes 10494976 | tf_op jit(solution)/shard_map/complement_update/dot_general | solution.py:23
  (113 shorter events, 15.3 us)
Async XLA Ops:
  7.2 100.3 %all-gather.2.cloned.1.call-start = ((), (), s32[]{:S(2)}) async-start(), calls=%async_computation | async-start | bytes 9437184 | tf_op jit(solution)/shard_map/gather_row_strip/all_gather | solution.py:91
  9.8 251.7 %all-reduce.3.cloned.1.call-start = ((), (), s32[]{:S(2)}) async-start(), calls=%async_computation.1 | async-start | bytes 17825792 | tf_op jit(solution)/shard_map/share_panel_rows/psum | solution.py:109
  15.8 0.7 copy-start.19
  107.4 2.6 copy-start.9
  129.8 0.7 copy-start.29
  281.8 0.8 copy-start.1
  302.0 2.0 copy-start.3
  304.1 1.4 copy-start
  320.0 0.7 copy-start.7
  323.8 62.6 %copy-start.13 = (f32[256,1024]{0,1:T(8,128)S(1)}, f32[256,1024]{0,1:T(8,128)}, u32[]{:S(2)}) copy-start(f32[256,1024]{0,1:T(8,128)} %get-tuple-element.27) | copy-start | bytes 3145732
  323.8 62.6 %copy-start.21 = (f32[65,1024]{0,1:T(8,128)S(1)}, f32[65,1024]{0,1:T(8,128)}, u32[]{:S(2)}) copy-start(f32[65,1024]{0,1:T(8,128)} %get-tuple-element.16) | copy-start | bytes 798724
  338.2 1.0 copy-start.10
  339.2 1.0 copy-start.14
  386.5 7.0 %copy-start.28 = (f32[256,128]{1,0:T(8,128)S(1)}, f32[256,128]{1,0:T(8,128)}, u32[]{:S(2)}) copy-start(f32[256,128]{1,0:T(8,128)} %blocked_cholesky_solve.8) | copy-start | bytes 393220
  386.5 10.3 %copy-start.2 = (f32[896,128]{1,0:T(8,128)S(1)}, f32[896,128]{1,0:T(8,128)}, u32[]{:S(2)}) copy-start(f32[896,128]{1,0:T(8,128)} %copy-done.1) | copy-start | bytes 1376260
  396.8 6.5 %copy-start.27 = (f32[256,128]{1,0:T(8,128)S(1)}, f32[256,128]{1,0:T(8,128)}, u32[]{:S(2)}) copy-start(f32[256,128]{1,0:T(8,128)} %blocked_cholesky_solve.9) | copy-start | bytes 393220
  396.8 8.8 %copy-start.4 = (f32[768,128]{1,0:T(8,128)S(1)}, f32[768,128]{1,0:T(8,128)}, u32[]{:S(2)}) copy-start(f32[768,128]{1,0:T(8,128)} %copy-done.3) | copy-start | bytes 1179652
  405.5 3.8 copy-start.26
  405.5 6.1 %copy-start.8 = (f32[640,128]{1,0:T(8,128)S(1)}, f32[640,128]{1,0:T(8,128)}, u32[]{:S(2)}) copy-start(f32[640,128]{1,0:T(8,128)} %copy-done.7) | copy-start | bytes 983044
  411.6 3.3 copy-start.25
  411.6 5.5 %copy-start.11 = (f32[512,128]{1,0:T(8,128)S(1)}, f32[512,128]{1,0:T(8,128)}, u32[]{:S(2)}) copy-start(f32[512,128]{1,0:T(8,128)} %copy-done.10) | copy-start | bytes 786436
  414.9 5.0 %copy-start.24 = (f32[256,128]{1,0:T(8,128)S(1)}, f32[256,128]{1,0:T(8,128)}, u32[]{:S(2)}) copy-start(f32[256,128]{1,0:T(8,128)} %blocked_cholesky_solve.12) | copy-start | bytes 393220
  417.1 5.0 %copy-start.5 = (f32[1345,128]{1,0:T(8,128)}, f32[1345,128]{1,0:T(8,128)S(1)}, u32[]{:S(2)}) copy-start(f32[1345,128]{1,0:T(8,128)S(1)} %get-tuple-element.46) | copy-start | bytes 2065924
  419.9 4.2 copy-start.23
  422.1 5.5 %copy-start.6 = (f32[1345,128]{1,0:T(8,128)}, f32[1345,128]{1,0:T(8,128)S(1)}, u32[]{:S(2)}) copy-start(f32[1345,128]{1,0:T(8,128)S(1)} %get-tuple-element.48) | copy-start | bytes 2065924
  422.1 5.5 %copy-start.22 = (f32[256,128]{1,0:T(8,128)S(1)}, f32[256,128]{1,0:T(8,128)}, u32[]{:S(2)}) copy-start(f32[256,128]{1,0:T(8,128)} %blocked_cholesky_solve.14) | copy-start | bytes 393220
  433.9 20.8 %copy-start.15 = (f32[1345,128]{0,1:T(8,128)S(1)}, f32[1345,128]{0,1:T(8,128)}, u32[]{:S(2)}) copy-start(f32[1345,128]{0,1:T(8,128)} %convolution_subtract_fusion.4) | copy-start | bytes 2065924
  438.5 21.9 %copy-start.32 = (f32[256]{0:T(256)S(1)}, f32[256]{0:T(256)}, u32[]{:S(2)}) copy-start(f32[256]{0:T(256)} %convert_element_type.57) | copy-start | bytes 3076
  438.5 22.1 %copy-start.33 = (f32[256]{0:T(256)S(1)}, f32[256]{0:T(256)}, u32[]{:S(2)}) copy-start(f32[256]{0:T(256)} %convert_element_type.58) | copy-start | bytes 3076
  440.7 21.3 %copy-start.16 = (f32[1345,128]{0,1:T(8,128)S(1)}, f32[1345,128]{0,1:T(8,128)}, u32[]{:S(2)}) copy-start(f32[1345,128]{0,1:T(8,128)} %copy.70) | copy-start | bytes 2065924
  440.7 21.3 %copy-start.17 = (f32[1345,128]{0,1:T(8,128)S(1)}, f32[1345,128]{0,1:T(8,128)}, u32[]{:S(2)}) copy-start(f32[1345,128]{0,1:T(8,128)} %copy.73) | copy-start | bytes 2065924
  440.7 21.3 %copy-start.30 = (pred[256]{0:T(512)(128)(4,1)S(1)}, pred[256]{0:T(512)(128)(4,1)}, u32[]{:S(2)}) copy-start(pred[256]{0:T(512)(128)(4,1)} %get-tuple-element.58) | copy-start | bytes 772
  440.8 21.3 %copy-start.31 = (pred[256]{0:T(512)(128)(4,1)S(1)}, pred[256]{0:T(512)(128)(4,1)}, u32[]{:S(2)}) copy-start(pred[256]{0:T(512)(128)(4,1)} %get-tuple-element.56) | copy-start | bytes 772
  441.9 20.2 %copy-start.18 = (f32[1345,128]{0,1:T(8,128)S(1)}, f32[1345,128]{0,1:T(8,128)}, u32[]{:S(2)}) copy-start(f32[1345,128]{0,1:T(8,128)} %copy.72) | copy-start | bytes 2065924
  441.9 20.2 %copy-start.20 = (f32[65,256]{0,1:T(8,128)S(1)}, f32[65,256]{0,1:T(8,128)}, u32[]{:S(2)}) copy-start(f32[65,256]{0,1:T(8,128)} %copy-done.19) | copy-start | bytes 199684
  441.9 20.2 %copy-start.34 = (pred[256]{0:T(512)(128)(4,1)S(1)}, pred[256]{0:T(512)(128)(4,1)}, u32[]{:S(2)}) copy-start(pred[256]{0:T(512)(128)(4,1)} %broadcast_compare_fusion.2) | copy-start | bytes 772
  462.0 4.5 copy-start.12
  462.1 4.5 copy-start.35
Sparse Core Ops, SparseCore 0:
  10.4 97.0 all-gather.1
  130.0 131.4 all-reduce.2
